TPU v7x, 256 devices: a whole 4x4x8 slice. The times are simulated.
256 devices in a mesh: seq: 16 (over y, x), fsdp: 16 (over z, core).
Axes of the slice: x: 4, y: 4, z: 8, core: 2. Of those that a mesh axis runs over, the one named last changes fastest.
Arguments:
- byte_rows: bfloat16 [16, 16384, 512], P('fsdp', 'seq'), may hold values from -6 to 6
- cotangent: bfloat16 [16, 16384, 512], P('fsdp', 'seq'), may hold values from -6 to 6
- doc_ids: int32 [16, 16384], P('fsdp', 'seq'), may hold values from 0 to 31, never falling along the last dimension, each value on 1 to 2048 neighbouring positions
- conv_weight: bfloat16 [8, 32, 16, 16], replicated, may hold values from -0.5 to 0.5
- norm_gain: float32 [512], replicated, may hold values from 0.5 to 1.5
- proj_weight: bfloat16 [4096, 512], P('fsdp'), may hold values from -0.25 to 0.25
- round_seed: int32 [1], replicated, may hold values from 0 to 1073741823
- step_count: int32 [1], replicated, may hold values from 0 to 999999
Outputs:
- grad_bytes: float32 [16, 16384, 512], P('fsdp', 'seq')
- grad_proj: float32 [4096, 512], P('fsdp')
- grad_conv: float32 [8, 32, 16, 16], replicated
- grad_gain: float32 [512], replicated
Inputs may be any that keep to these rules, and one draw needn't show every extreme that they name: `doc_ids`: along each sequence the document numbers never fall; no document covers more than 2048 bytes, and one covers exactly 2048.
All inputs are finite; a program needn't handle non-finite values.
Results may differ from a plain program's by a relative error of at most 0.0046.
Values may be sent and summed in bfloat16 or wider, within the bound.
No kernel may reach another device: no remote copies, remote signals or barrier semaphores. Data moves between devices by JAX's collectives and lax.ppermute only.
A program may use at most 128 MiB of HBM per device.

v0:
```python
import math
import jax
import jax.numpy as jnp
from jax import lax
from jax.sharding import PartitionSpec as P

GROUPS = 32
KERNEL = 8
STRIDE = 4
CG = 16
GELU_A = 0.7978845608028654
GELU_B = 0.044715
QUANT = 0.25


def shifted(value, axis, steps):
    count = lax.axis_size(axis)
    initial, last = (max(0, -steps), min(count, count - steps))
    return lax.ppermute(value, axis, [(source, source + steps) for source in range(initial, last)])


def gelu_grad(values):
    tangent = jnp.tanh(GELU_A * (values + GELU_B * values * values * values))
    return 0.5 * (1.0 + tangent) + 0.5 * values * (1.0 - tangent * tangent) * GELU_A * (
        1.0 + 3.0 * GELU_B * values * values
    )


def mix_bits(flat_index, seed_value, step_value):
    hashed = (
        flat_index * jnp.int32(-1640531535)
        + seed_value * jnp.int32(-2048144777)
        + step_value * jnp.int32(-1028477379)
    )
    hashed = hashed ^ lax.shift_right_logical(hashed, jnp.int32(16))
    hashed = hashed * jnp.int32(2146121005)
    hashed = hashed ^ lax.shift_right_logical(hashed, jnp.int32(15))
    hashed = hashed * jnp.int32(-2073254261)
    hashed = hashed ^ lax.shift_right_logical(hashed, jnp.int32(16))
    return lax.shift_right_logical(hashed, jnp.int32(8)).astype(jnp.float32) / 16777216.0


def tap_windows(series, extra_rows, patches):
    joined = jnp.concatenate([series, extra_rows], 0)
    tail_shape = joined.shape[1:]
    lower = joined[:-STRIDE].reshape((patches, STRIDE) + tail_shape)
    upper = joined[STRIDE:].reshape((patches, STRIDE) + tail_shape)
    return jnp.concatenate([lower, upper], 1)


def per_device(
    byte_rows, cotangent, doc_ids, conv_weight, norm_gain, proj_weight, round_seed, step_count
):
    byte_block = byte_rows[0]
    upstream = cotangent[0]
    doc_block = doc_ids[0]
    length = byte_block.shape[0]
    row_width = byte_block.shape[1]
    patches = length // STRIDE
    panel_rows = proj_weight.shape[0]
    full_width = panel_rows * lax.axis_size("fsdp")
    next_bytes, next_up, next_docs = shifted(
        (byte_block[:STRIDE], upstream[:STRIDE], doc_block[:STRIDE]), "seq", -1
    )
    window = tap_windows(byte_block, next_bytes, patches)
    up_window = tap_windows(upstream, next_up, patches)
    doc_window = tap_windows(doc_block, next_docs, patches)
    is_last = lax.axis_index("seq") == lax.axis_size("seq") - 1
    patch_ids = lax.broadcasted_iota(jnp.int32, (patches, KERNEL), 0)
    tap_ids = lax.broadcasted_iota(jnp.int32, (patches, KERNEL), 1)
    spilled = is_last & (patch_ids == patches - 1) & (tap_ids >= STRIDE)
    keep_tap = (doc_window == doc_window[:, :1]) & jnp.logical_not(spilled)
    keep_f = keep_tap.astype(jnp.float32)[:, :, None]
    masked = window * keep_tap.astype(jnp.bfloat16)[:, :, None]
    grouped = masked.reshape(patches, KERNEL, GROUPS, CG)
    hidden = jnp.einsum(
        "pkgc,kgcd->pgd", grouped, conv_weight, preferred_element_type=jnp.float32
    ).reshape(patches, row_width)
    factor = lax.rsqrt(jnp.mean(hidden * hidden, axis=-1, keepdims=True) + 1e-06)
    normed = (hidden * factor * norm_gain).astype(jnp.bfloat16)
    contract_last = (((1,), (1,)), ((), ()))
    full_proj = lax.all_gather(proj_weight, "fsdp", axis=0, tiled=True)
    pre_act = lax.dot_general(normed, full_proj, contract_last, preferred_element_type=jnp.float32)
    grad_pre = (
        up_window.astype(jnp.float32)
        * keep_f
        * gelu_grad(pre_act.reshape(patches, KERNEL, row_width))
    )
    grad_pre = grad_pre.reshape(patches, full_width).astype(jnp.bfloat16)
    grad_norm = jnp.dot(grad_pre, full_proj, preferred_element_type=jnp.float32)
    contract_first = (((0,), (0,)), ((), ()))
    panel_part = lax.psum_scatter(
        lax.dot_general(grad_pre, normed, contract_first, preferred_element_type=jnp.float32),
        "fsdp",
        scatter_dimension=0,
        tiled=True,
    )
    proj_sum = lax.psum(panel_part, "seq")
    gain_part = jnp.sum(grad_norm * hidden * factor, axis=0)
    gained = norm_gain * grad_norm
    grad_hidden = factor * gained - hidden * factor * factor * factor * jnp.mean(
        gained * hidden, axis=-1, keepdims=True
    )
    grad_hidden = grad_hidden.reshape(patches, GROUPS, CG)
    grouped_f = grouped.astype(jnp.float32)
    conv_f = conv_weight.astype(jnp.float32)
    conv_part = jnp.einsum(
        "pkgc,pgd->kgcd", grouped_f, grad_hidden, precision=lax.Precision.HIGHEST
    )
    gain_sum, conv_sum = lax.psum((gain_part, conv_part), ("seq", "fsdp"))
    grad_window = jnp.einsum("pgd,kgcd->pkgc", grad_hidden, conv_f, precision=lax.Precision.HIGHEST)
    grad_window = grad_window.reshape(patches, KERNEL, row_width) * keep_f
    back_lower = grad_window[:, :STRIDE].reshape(length, row_width)
    back_upper = grad_window[:, STRIDE:].reshape(length, row_width)
    incoming = shifted(back_upper[length - STRIDE :], "seq", 1)
    back_rows = back_lower + jnp.concatenate([incoming, back_upper[: length - STRIDE]], 0)
    grad_bytes = (upstream.astype(jnp.float32) + back_rows)[None]
    total_patches = patches * lax.axis_size("seq") * lax.axis_size("fsdp")
    grad_scale = 1.0 / math.sqrt(total_patches)
    first_panel = lax.axis_index("fsdp") * jnp.int32(panel_rows)
    row_index = first_panel + jnp.arange(panel_rows, dtype=jnp.int32)
    flat_index = (
        row_index[:, None] * jnp.int32(row_width) + jnp.arange(row_width, dtype=jnp.int32)[None, :]
    )
    dither_noise = mix_bits(flat_index, round_seed[0], step_count[0])
    grad_proj = proj_sum * grad_scale + QUANT * (dither_noise - 0.5)
    return (grad_bytes, grad_proj, conv_sum * grad_scale, gain_sum * grad_scale)


def solution(mesh):
    in_specs = (
        P("fsdp", "seq", None),
        P("fsdp", "seq", None),
        P("fsdp", "seq"),
        P(),
        P(),
        P("fsdp", None),
        P(),
        P(),
    )
    out_specs = (P("fsdp", "seq", None), P("fsdp", None), P(), P())
    return jax.shard_map(
        per_device, mesh=mesh, in_specs=in_specs, out_specs=out_specs, check_vma=False
    )
```

profile of v0, /device:TPU:32, one launch (start us, length us, event | category | flops | bytes accessed | tf_op | source)
XLA Modules:
  0.0 572.1 jit_solution(2157465076530851833)
XLA Ops:
  7.2 0.7 all-gather.2.cloned.1.call-update
  7.9 0.7 slice_bitcast_fusion.2
  8.6 1.3 collective-permute-start.1
  9.9 0.7 slice_bitcast_fusion.1
  10.6 1.3 collective-permute-start
  11.9 0.7 slice_bitcast_fusion
  12.6 1.3 collective-permute-start.2
  13.9 9.7 %concatenate.46 = bf16[256,4,32,16]{3,2,1,0:T(8,128)(2,1)} reshape(bf16[1,1024,512]{2,1,0:T(8,128)(2,1)} %param.8) | data formatting | bytes 2097152 | tf_op jit(solution)/shard_map/concatenate | solution.py:48
  23.8 0.5 broadcast.145
  24.4 0.7 reduce.6
  25.2 9.8 %copy.43 = bf16[256,4,32,16]{0,3,2,1:T(8,128)(2,1)} copy(bf16[256,4,32,16]{3,2,1,0:T(8,128)(2,1)} %concatenate.46) | data formatting | bytes 2097152 | tf_op jit(solution)/shard_map/concatenate | solution.py:48
  35.0 3.1 copy.65
  38.2 1.2 copy.49
  40.2 8.2 %concatenate.48 = bf16[256,4,32,16]{3,2,1,0:T(8,128)(2,1)} reshape(bf16[1024,512]{1,0:T(8,128)(2,1)S(1)} %pad_maximum_fusion.1) | data formatting | bytes 2097152 | tf_op jit(solution)/shard_map/concatenate | solution.py:48
  48.4 9.8 %copy.44 = bf16[256,4,32,16]{0,3,2,1:T(8,128)(2,1)} copy(bf16[256,4,32,16]{3,2,1,0:T(8,128)(2,1)} %concatenate.48) | data formatting | bytes 2097152 | tf_op jit(solution)/shard_map/concatenate | solution.py:48
  58.8 1.2 copy.50
  60.9 1.0 copy-done.8
  61.9 0.8 fusion.21
  62.7 0.8 copy-done.4
  63.6 7.9 %fusion.6 = bf16[256,8,512]{2,0,1:T(8,128)(2,1)} fusion(bf16[256,512,1]{0,1,2:T(8,128)(2,1)S(1)} %bitcast.62, bf16[8,512,512]{2,1,0:T(8,128)(2,1)} %bitcast.67, bf16[256,4,512]{2,0,1:T(8,128)(2,1)} %copy.50, bf16[256,4,512]{2,0,1:T(8,128)(2,1)} %copy.49, f32[256,8]{0,1:T(8,128)S(1)} %get-tuple-element.18), kind=kOutput, calls=%fused_computation.8 | convolution fusion | flops 1096810496 | bytes 8658944 | tf_op jit(solution)/shard_map/dot_general | solution.py:83
  71.5 3.9 copy.52
  75.4 6.1 %fusion.27 = f32[4096,512]{1,0:T(8,128)} fusion(bf16[256,4096]{0,1:T(8,128)(2,1)} %bitcast.55, bf16[256,512]{0,1:T(8,128)(2,1)S(1)} %bitcast.63), kind=kOutput, calls=%fused_computation.54 | convolution fusion | flops 1073741824 | bytes 10747904 | tf_op jit(solution)/shard_map/dot_general | solution.py:93
  81.8 3.5 copy.56
  86.6 2.0 copy.53
  88.7 4.3 multiply_reduce_fusion
  93.1 1.0 multiply_subtract_fusion
  94.0 2.0 copy.55
  96.1 3.2 convolution_bitcast_fusion
  99.2 2.6 copy.57
  101.8 5.4 copy.58
  107.2 2.6 broadcast_multiply_fusion
  109.8 2.0 copy-done
  111.8 5.8 %collective-permute-start.3 = (f32[4,512]{1,0:T(4,128)S(1)}, f32[4,512]{1,0:T(4,128)S(1)}, u32[]{:S(2)}, u32[]{:S(2)}) collective-permute-start(f32[4,512]{1,0:T(4,128)S(1)} %bitcast.65), channel_id=1, source_target_pairs={{0,16},{16,32},{32,48},{48,64},{64,80},{80,96},{96,112},{112,128},... | collective-permute-start | bytes 24584 | tf_op jit(solution)/shard_map/ppermute | solution.py:19
  117.6 82.1 %psum.23 = f32[512]{0:T(512)S(1)} all-reduce(f32[512]{0:T(512)S(1)} %get-tuple-element.16), channel_id=1, replica_groups=mesh['seq'=16,'fsdp'=16] {'seq','fsdp'}, use_global_device_ids=true, to_apply=%region_6.0 | all-reduce | flops 512 | bytes 4096 | tf_op jit(solution)/shard_map/psum | solution.py:110
  199.7 9.8 %fusion.10 = f32[8,32,16,16]{2,3,0,1:T(8,128)} fusion(f32[256,32,16,1]{0,2,3,1:T(8,128)} %bitcast.60, bf16[256,8,32,16]{0,3,2,1:T(8,128)(2,1)S(1)} %maximum_multiply_fusion), kind=kOutput, calls=%fused_computation.16 | convolution fusion | flops 201326592 | bytes 2883584 | tf_op jit(solution)/shard_map/pkgc,pgd->kgcd/dot_general | solution.py:107
  209.8 0.6 broadcast_multiply_fusion.2
  210.4 2.2 copy-done.1
  212.7 1.4 slice-done
  214.2 2.7 copy.59
  216.8 2.9 reshape.243
  219.8 2.7 copy.60
  222.4 3.1 concatenate.56
  225.6 3.5 fusion.7
  229.1 234.9 %all-reduce.5.cloned.1.call-done = f32[8,32,16,16]{2,3,0,1:T(8,128)} async-done(((f32[8,32,16,16]{2,3,0,1:T(8,128)}), f32[8,32,16,16]{2,3,0,1:T(8,128)}) %all-reduce.5.cloned.1.call-update) | async-done | bytes 262160 | tf_op jit(solution)/shard_map/psum | solution.py:110
  464.1 1.8 broadcast_multiply_fusion.1
  465.8 2.3 copy.63
  468.1 95.2 %all-reduce.3.cloned.1.call-done = f32[256,512]{1,0:T(8,128)} async-done(((f32[256,512]{1,0:T(8,128)}), f32[256,512]{1,0:T(8,128)}) %all-reduce.3.cloned.1.call-update) | async-done | bytes 524304 | tf_op jit(solution)/shard_map/psum | solution.py:98
  563.3 2.2 fusion.20
  (57 shorter events, 3.8 us)
Async XLA Ops:
  7.2 56.5 %all-gather.2.cloned.1.call-start = ((), (), s32[]{:S(2)}) async-start(), calls=%async_computation.1 | async-start | bytes 4456448 | tf_op jit(solution)/shard_map/all_gather | solution.py:82
  7.9 217.7 %reduce-scatter.2.cloned.1.call-start = ((), (), s32[]{:S(2)}) async-start(), calls=%async_computation.2 | async-start | bytes 8912896 | tf_op jit(solution)/shard_map/reduce_scatter | solution.py:92
  8.6 30.9 %collective-permute-start.1 = (s32[4]{0:T(128)S(1)}, s32[4]{0:T(128)S(1)}, u32[]{:S(2)}, u32[]{:S(2)}) collective-permute-start(s32[4]{0:T(128)S(1)} %slice_bitcast_fusion.2), channel_id=1, source_target_pairs={{16,0},{32,16},{48,32},{64,48},{80,64},{96,80},{112,96},{128,112},... | collective-permute-start | bytes 56 | tf_op jit(solution)/shard_map/ppermute | solution.py:19
  10.6 29.3 %collective-permute-start = (bf16[4,512]{1,0:T(4,128)(2,1)S(1)}, bf16[4,512]{1,0:T(4,128)(2,1)S(1)}, u32[]{:S(2)}, u32[]{:S(2)}) collective-permute-start(bf16[4,512]{1,0:T(4,128)(2,1)S(1)} %slice_bitcast_fusion.1), channel_id=1, source_target_pairs={{16,0},{32,16},{48,32},{64,48},{80,64},{96,80},{112,96},{128,112},... | collective-permute-start | bytes 12296 | tf_op jit(solution)/shard_map/ppermute | solution.py:19
  12.6 45.6 %collective-permute-start.2 = (bf16[4,512]{1,0:T(4,128)(2,1)S(1)}, bf16[4,512]{1,0:T(4,128)(2,1)S(1)}, u32[]{:S(2)}, u32[]{:S(2)}) collective-permute-start(bf16[4,512]{1,0:T(4,128)(2,1)S(1)} %slice_bitcast_fusion), channel_id=1, source_target_pairs={{16,0},{32,16},{48,32},{64,48},{80,64},{96,80},{112,96},{128,112},... | collective-permute-start | bytes 12296 | tf_op jit(solution)/shard_map/ppermute | solution.py:19
  13.9 9.7 %copy-start.2 = (bf16[1,1024,512]{2,1,0:T(8,128)(2,1)S(1)}, bf16[1,1024,512]{2,1,0:T(8,128)(2,1)}, u32[]{:S(2)}) copy-start(bf16[1,1024,512]{2,1,0:T(8,128)(2,1)} %param.9) | copy-start | bytes 3145732
  23.6 0.8 copy-start.10
  25.2 12.9 %copy-start.11 = (f32[512]{0:T(512)S(1)}, f32[512]{0:T(512)}, u32[]{:S(2)}) copy-start(f32[512]{0:T(512)} %param.12) | copy-start | bytes 6148
  35.0 4.9 copy-start.5
  58.8 1.4 copy-start.6
  58.8 1.9 copy-start.7
  60.7 1.2 copy-start.8
  62.7 0.8 copy-start.4
  81.6 382.5 %all-reduce.5.cloned.1.call-start = ((), (), s32[]{:S(2)}) async-start(), calls=%async_computation.4 | async-start | bytes 4194304 | tf_op jit(solution)/shard_map/psum | solution.py:110
  88.7 4.4 copy-start.9
  109.8 2.0 copy-start
  111.8 113.8 %collective-permute-start.3 = (f32[4,512]{1,0:T(4,128)S(1)}, f32[4,512]{1,0:T(4,128)S(1)}, u32[]{:S(2)}, u32[]{:S(2)}) collective-permute-start(f32[4,512]{1,0:T(4,128)S(1)} %bitcast.65), channel_id=1, source_target_pairs={{0,16},{16,32},{32,48},{48,64},{64,80},{80,96},{96,112},{112,128},... | collective-permute-start | bytes 24584 | tf_op jit(solution)/shard_map/ppermute | solution.py:19
  209.5 353.8 %all-reduce.3.cloned.1.call-start = ((), (), s32[]{:S(2)}) async-start(), calls=%async_computation.3 | async-start | bytes 1048576 | tf_op jit(solution)/shard_map/psum | solution.py:98
  210.4 2.2 copy-start.1
  212.6 1.6 slice-start
  222.4 3.2 copy-start.3
Sparse Core Ops, SparseCore 0:
  9.8 44.4 all-gather.1
  81.7 75.4 reduce-scatter.1
  209.6 254.3 all-reduce.4
  467.1 96.1 all-reduce.2
where the time goes:
time: 574 us; the launch traced here: 572 us
  waiting for transfers between devices  331 us (58%)
  local copies, waits for them, and re-layouts  88.1 us (15%)
  blocking collectives  82.1 us (14%)
  matrix products  32.1 us (6%)
  between operations  15.3 us (3%)
  other arithmetic  13.3 us (2%)
  starting transfers between devices  10.2 us (2%)
    psum x1, waiting for transfers between devices, per_device(): gain_sum, conv_sum = lax.psum((gain_part, conv_part), ('seq', 'fsdp'))  235 us
    psum x1, waiting for transfers between devices, per_device(): proj_sum = lax.psum(panel_part, 'seq')  95.2 us
    psum x1, blocking collectives, per_device(): gain_sum, conv_sum = lax.psum((gain_part, conv_part), ('seq', 'fsdp'))  82.1 us
    concatenate x6, local copies, waits for them, and re-layouts, tap_windows(): return jnp.concatenate([lower, upper], 1)  37.7 us
    unnamed x29, local copies, waits for them, and re-layouts  16.2 us
  transfers between devices with their start and end apart: 8, of which 2 were waited for; matrix products, arithmetic and copies ran while one was open for 18% of the time, Pallas kernels for 0%

commit v1 on v0

--- a/solution.py
+++ b/solution.py
@@ -107,7 +107,7 @@
     conv_part = jnp.einsum(
         "pkgc,pgd->kgcd", grouped_f, grad_hidden, precision=lax.Precision.HIGHEST
     )
-    gain_sum, conv_sum = lax.psum((gain_part, conv_part), ("seq", "fsdp"))
+    gain_sum, conv_sum = lax.psum(lax.psum((gain_part, conv_part), "seq"), "fsdp")
     grad_window = jnp.einsum("pgd,kgcd->pkgc", grad_hidden, conv_f, precision=lax.Precision.HIGHEST)
     grad_window = grad_window.reshape(patches, KERNEL, row_width) * keep_f
     back_lower = grad_window[:, :STRIDE].reshape(length, row_width)

time: 574 us -> 396 us (0.69)
  waiting for transfers between devices: 331 us -> 171 us
  blocking collectives: 82.1 us -> 62.8 us
    psum x1, waiting for transfers between devices: 235 us -> 112 us  [per_device(): lax.psum(lax.psum((gain_part, conv_part), 'seq'), 'fsdp')]
    psum x1, waiting for transfers between devices: 95.2 us -> 18.9 us  [per_device(): proj_sum = lax.psum(panel_part, 'seq')]
    reduce_scatter x1, waiting for transfers between devices: 0.01 us -> 40 us  [per_device(): lax.psum_scatter(lax.dot_general(grad_pre, normed, contract_first, prefer...]
    psum x1 -> x2, blocking collectives: 82.1 us -> 62.8 us  [the longest x1 38.4 us: per_device(): lax.psum((gain_part, conv_part), 'seq')]
    unnamed x29 -> x31, local copies, waits for them, and re-layouts: 16.2 us -> 17.2 us
  transfers between devices with their start and end apart: 8 -> 8, of which waited for: 2 -> 3; matrix products, arithmetic and copies ran while one was open for 18% -> 26% of each run, Pallas kernels for 0% -> 0%
where the time goes in v1:
time: 396 us; the launch traced here: 390 us
  waiting for transfers between devices  171 us (43%)
  local copies, waits for them, and re-layouts  89.2 us (23%)
  blocking collectives  62.8 us (16%)
  matrix products  32.1 us (8%)
  between operations  15.3 us (4%)
  other arithmetic  12.2 us (3%)
  starting transfers between devices  7.56 us (2%)
    psum x1, waiting for transfers between devices, per_device(): lax.psum(lax.psum((gain_part, conv_part), 'seq'), 'fsdp')  112 us
    reduce_scatter x1, waiting for transfers between devices, per_device(): lax.psum_scatter(lax.dot_general(grad_pre, normed, contract_first, prefer...  40 us
    psum x1, blocking collectives, per_device(): lax.psum((gain_part, conv_part), 'seq')  38.4 us
    concatenate x6, local copies, waits for them, and re-layouts, tap_windows(): return jnp.concatenate([lower, upper], 1)  37.7 us
    psum x1, blocking collectives, per_device(): lax.psum(lax.psum((gain_part, conv_part), 'seq'), 'fsdp')  24.4 us
    psum x1, waiting for transfers between devices, per_device(): proj_sum = lax.psum(panel_part, 'seq')  18.9 us
    unnamed x31, local copies, waits for them, and re-layouts  17.2 us
    dot_general x1, matrix products, per_device(): jnp.einsum('pkgc,pgd->kgcd', grouped_f, grad_hidden, precision=lax.Precis...  9.8 us
  transfers between devices with their start and end apart: 8, of which 3 were waited for; matrix products, arithmetic and copies ran while one was open for 26% of the time, Pallas kernels for 0%

profile of v1, /device:TPU:32, one launch (start us, length us, event | category | flops | bytes accessed | tf_op | source)
XLA Modules:
  0.0 390.5 jit_solution(13249032405443954988)
XLA Ops:
  7.2 0.7 all-gather.2.cloned.1.call-update
  8.6 1.3 collective-permute-start.1
  9.9 0.7 slice_bitcast_fusion.1
  10.6 1.3 collective-permute-start
  11.9 0.7 slice_bitcast_fusion
  12.6 1.3 collective-permute-start.2
  13.9 9.7 %concatenate.46 = bf16[256,4,32,16]{3,2,1,0:T(8,128)(2,1)} reshape(bf16[1,1024,512]{2,1,0:T(8,128)(2,1)} %param.8) | data formatting | bytes 2097152 | tf_op jit(solution)/shard_map/concatenate | solution.py:48
  24.4 0.7 reduce.6
  25.2 9.8 %copy.43 = bf16[256,4,32,16]{0,3,2,1:T(8,128)(2,1)} copy(bf16[256,4,32,16]{3,2,1,0:T(8,128)(2,1)} %concatenate.46) | data formatting | bytes 2097152 | tf_op jit(solution)/shard_map/concatenate | solution.py:48
  35.0 3.1 copy.65
  38.2 1.2 copy.49
  40.2 8.2 %concatenate.48 = bf16[256,4,32,16]{3,2,1,0:T(8,128)(2,1)} reshape(bf16[1024,512]{1,0:T(8,128)(2,1)S(1)} %pad_maximum_fusion.1) | data formatting | bytes 2097152 | tf_op jit(solution)/shard_map/concatenate | solution.py:48
  48.4 9.8 %copy.44 = bf16[256,4,32,16]{0,3,2,1:T(8,128)(2,1)} copy(bf16[256,4,32,16]{3,2,1,0:T(8,128)(2,1)} %concatenate.48) | data formatting | bytes 2097152 | tf_op jit(solution)/shard_map/concatenate | solution.py:48
  58.8 1.2 copy.50
  60.9 1.0 copy-done.8
  61.9 0.8 fusion.21
  62.7 0.8 copy-done.4
  63.6 7.9 %fusion.6 = bf16[256,8,512]{2,0,1:T(8,128)(2,1)} fusion(bf16[256,512,1]{0,1,2:T(8,128)(2,1)S(1)} %bitcast.62, bf16[8,512,512]{2,1,0:T(8,128)(2,1)} %bitcast.67, bf16[256,4,512]{2,0,1:T(8,128)(2,1)} %copy.50, bf16[256,4,512]{2,0,1:T(8,128)(2,1)} %copy.49, f32[256,8]{0,1:T(8,128)S(1)} %get-tuple-element.20), kind=kOutput, calls=%fused_computation.8 | convolution fusion | flops 1096810496 | bytes 8658944 | tf_op jit(solution)/shard_map/dot_general | solution.py:83
  71.5 3.9 copy.52
  75.4 6.1 %fusion.27 = f32[4096,512]{1,0:T(8,128)} fusion(bf16[256,4096]{0,1:T(8,128)(2,1)} %bitcast.55, bf16[256,512]{0,1:T(8,128)(2,1)S(1)} %bitcast.63), kind=kOutput, calls=%fused_computation.54 | convolution fusion | flops 1073741824 | bytes 10747904 | tf_op jit(solution)/shard_map/dot_general | solution.py:93
  81.8 3.5 copy.56
  86.7 2.0 copy.53
  88.7 4.3 %multiply_reduce_fusion = (f32[512]{0:T(512)S(1)}, f32[256]{0:T(256)S(1)}, f32[256,512]{1,0:T(8,128)S(1)}) fusion(f32[256,512]{1,0:T(8,128)} %copy.53, f32[256]{0:T(256)S(1)} %add_rsqrt_fusion, f32[512]{0:T(512)S(1)} %copy-done.12, bf16[256,4096]{0,1:T(8,128)(2,1)} %bitcast.56, bf16[4096,512]{1,0:T(8,128)(2,1)} %all-gather.2.cloned.1.call-done), kind=kOutput, calls=%fused_computation.36 | convolution fusion | flops 1074527488 | bytes 7346176 | tf_op jit(solution)/shard_map/dot_general | solution.py:90
  93.1 1.0 multiply_subtract_fusion
  94.0 2.0 copy.55
  96.1 3.2 convolution_bitcast_fusion
  99.2 2.6 copy.57
  101.8 5.4 %copy.58 = f32[256,8,512]{2,0,1:T(8,128)} copy(f32[256,8,512]{0,2,1:T(8,128)} %bitcast.54) | data formatting | bytes 8388608 | tf_op jit(solution)/shard_map/reshape | solution.py:112
  107.2 9.8 %fusion.10 = f32[8,32,16,16]{2,3,0,1:T(8,128)} fusion(f32[256,32,16,1]{0,2,3,1:T(8,128)} %bitcast.60, bf16[256,8,32,16]{0,3,2,1:T(8,128)(2,1)S(1)} %maximum_multiply_fusion), kind=kOutput, calls=%fused_computation.16 | convolution fusion | flops 201326592 | bytes 2883584 | tf_op jit(solution)/shard_map/pkgc,pgd->kgcd/dot_general | solution.py:107
  117.0 40.0 %reduce-scatter.2.cloned.1.call-done = f32[256,512]{1,0:T(8,128)} async-done(((f32[4096,512]{1,0:T(8,128)}), f32[256,512]{1,0:T(8,128)}) %reduce-scatter.2.cloned.1.call-update) | async-done | bytes 524304 | tf_op jit(solution)/shard_map/reduce_scatter | solution.py:92
  157.1 2.5 broadcast_multiply_fusion
  159.6 1.9 copy-done
  161.6 3.4 collective-permute-start.3
  165.0 38.4 %psum.38 = f32[512]{0:T(512)S(1)} all-reduce(f32[512]{0:T(512)S(1)} %get-tuple-element.16), channel_id=1, replica_groups=mesh['seq'=16,'fsdp'=16] {'seq'}, use_global_device_ids=true, to_apply=%region_7.0 | all-reduce | flops 512 | bytes 4096 | tf_op jit(solution)/shard_map/psum | solution.py:110
  203.4 24.4 %psum.39 = f32[512]{0:T(512)S(1)} all-reduce(f32[512]{0:T(512)S(1)} %psum.38), channel_id=1, replica_groups=mesh['seq'=16,'fsdp'=16] {'fsdp'}, use_global_device_ids=true, to_apply=%region_8.0 | all-reduce | flops 512 | bytes 4096 | tf_op jit(solution)/shard_map/psum | solution.py:110
  228.4 2.2 copy-done.1
  230.8 1.4 slice-done
  232.2 2.7 copy.59
  234.9 3.0 reshape.243
  237.9 2.7 copy.60
  240.5 3.1 concatenate.56
  243.6 3.5 fusion.7
  247.1 18.9 %all-reduce.6.cloned.1.call-done = (f32[256,512]{1,0:T(8,128)}, f32[8,32,16,16]{2,3,0,1:T(8,128)}) async-done(((f32[256,512]{1,0:T(8,128)}, f32[8,32,16,16]{2,3,0,1:T(8,128)}), (f32[256,512]{1,0:T(8,128)}, f32[8,32,16,16]{2,3,0,1:T(8,128)})) %all-reduce.6.cloned.1.call-update) | async-done | bytes 786448 | tf_op jit(solution)/shard_map/psum | solution.py:98
  266.1 1.0 copy-done.10
  267.1 1.2 fusion.20
  268.3 111.6 %all-reduce.4.cloned.1.call-done = f32[8,32,16,16]{2,3,0,1:T(8,128)} async-done(((f32[8,32,16,16]{2,3,0,1:T(8,128)}), f32[8,32,16,16]{2,3,0,1:T(8,128)}) %all-reduce.4.cloned.1.call-update) | async-done | bytes 262160 | tf_op jit(solution)/shard_map/psum | solution.py:110
  379.9 1.8 broadcast_multiply_fusion.1
  381.7 2.3 copy.63
  (60 shorter events, 5.3 us)
Async XLA Ops:
  7.2 56.5 %all-gather.2.cloned.1.call-start = ((), (), s32[]{:S(2)}) async-start(), calls=%async_computation.1 | async-start | bytes 4456448 | tf_op jit(solution)/shard_map/all_gather | solution.py:82
  7.9 149.1 %reduce-scatter.2.cloned.1.call-start = ((), (), s32[]{:S(2)}) async-start(), calls=%async_computation.2 | async-start | bytes 8912896 | tf_op jit(solution)/shard_map/reduce_scatter | solution.py:92
  8.6 30.9 %collective-permute-start.1 = (s32[4]{0:T(128)S(1)}, s32[4]{0:T(128)S(1)}, u32[]{:S(2)}, u32[]{:S(2)}) collective-permute-start(s32[4]{0:T(128)S(1)} %slice_bitcast_fusion.2), channel_id=1, source_target_pairs={{16,0},{32,16},{48,32},{64,48},{80,64},{96,80},{112,96},{128,112},... | collective-permute-start | bytes 56 | tf_op jit(solution)/shard_map/ppermute | solution.py:19
  10.6 29.3 %collective-permute-start = (bf16[4,512]{1,0:T(4,128)(2,1)S(1)}, bf16[4,512]{1,0:T(4,128)(2,1)S(1)}, u32[]{:S(2)}, u32[]{:S(2)}) collective-permute-start(bf16[4,512]{1,0:T(4,128)(2,1)S(1)} %slice_bitcast_fusion.1), channel_id=1, source_target_pairs={{16,0},{32,16},{48,32},{64,48},{80,64},{96,80},{112,96},{128,112},... | collective-permute-start | bytes 12296 | tf_op jit(solution)/shard_map/ppermute | solution.py:19
  12.6 45.6 %collective-permute-start.2 = (bf16[4,512]{1,0:T(4,128)(2,1)S(1)}, bf16[4,512]{1,0:T(4,128)(2,1)S(1)}, u32[]{:S(2)}, u32[]{:S(2)}) collective-permute-start(bf16[4,512]{1,0:T(4,128)(2,1)S(1)} %slice_bitcast_fusion), channel_id=1, source_target_pairs={{16,0},{32,16},{48,32},{64,48},{80,64},{96,80},{112,96},{128,112},... | collective-permute-start | bytes 12296 | tf_op jit(solution)/shard_map/ppermute | solution.py:19
  13.9 9.7 %copy-start.2 = (bf16[1,1024,512]{2,1,0:T(8,128)(2,1)S(1)}, bf16[1,1024,512]{2,1,0:T(8,128)(2,1)}, u32[]{:S(2)}) copy-start(bf16[1,1024,512]{2,1,0:T(8,128)(2,1)} %param.9) | copy-start | bytes 3145732
  23.6 0.8 copy-start.11
  25.2 12.9 %copy-start.12 = (f32[512]{0:T(512)S(1)}, f32[512]{0:T(512)}, u32[]{:S(2)}) copy-start(f32[512]{0:T(512)} %param.12) | copy-start | bytes 6148
  35.0 4.9 %copy-start.5 = (bf16[1,1024,512]{2,1,0:T(8,128)(2,1)S(1)}, bf16[1,1024,512]{2,1,0:T(8,128)(2,1)}, u32[]{:S(2)}) copy-start(bf16[1,1024,512]{2,1,0:T(8,128)(2,1)} %param.8) | copy-start | bytes 3145732
  58.8 1.4 copy-start.6
  58.8 1.9 copy-start.7
  60.7 1.2 copy-start.8
  62.7 0.8 copy-start.4
  81.6 184.5 %all-reduce.6.cloned.1.call-start = ((), (), s32[]{:S(2)}) async-start(), calls=%async_computation.4 | async-start | bytes 5242880 | tf_op jit(solution)/shard_map/psum | solution.py:98
  88.7 4.4 %copy-start.9 = (f32[256,512]{1,0:T(8,128)S(1)}, f32[256,512]{1,0:T(8,128)}, u32[]{:S(2)}) copy-start(f32[256,512]{1,0:T(8,128)} %copy.53) | copy-start | bytes 1572868
  157.0 222.8 %all-reduce.4.cloned.1.call-start = ((), (), s32[]{:S(2)}) async-start(), calls=%async_computation.3 | async-start | bytes 4194304 | tf_op jit(solution)/shard_map/psum | solution.py:110
  159.6 1.9 copy-start
  161.6 82.0 %collective-permute-start.3 = (f32[4,512]{1,0:T(4,128)S(1)}, f32[4,512]{1,0:T(4,128)S(1)}, u32[]{:S(2)}, u32[]{:S(2)}) collective-permute-start(f32[4,512]{1,0:T(4,128)S(1)} %bitcast.65), channel_id=1, source_target_pairs={{0,16},{16,32},{32,48},{48,64},{64,80},{80,96},{96,112},{112,128},... | collective-permute-start | bytes 24584 | tf_op jit(solution)/shard_map/ppermute | solution.py:19
  228.4 2.2 copy-start.1
  230.6 1.6 slice-start
  240.5 3.1 copy-start.3
  266.0 1.0 copy-start.10
Sparse Core Ops, SparseCore 0:
  9.8 44.4 all-gather.1
  81.7 75.2 reduce-scatter.1
  160.4 105.5 all-reduce.5
  268.4 111.4 all-reduce.3
